TPU v7x, 256 devices: a whole 4x4x8 slice. The times are simulated.
256 devices in a mesh: dp: 64 (over z, x, core), mp: 4 (over y).
Axes of the slice: x: 4, y: 4, z: 8, core: 2. Of those that a mesh axis runs over, the one named last changes fastest.
Arguments:
- embed_table: float32 [16, 32768, 256], P('mp', 'dp'), may hold values from -5 to 5
- accum: float32 [16, 32768], P('mp', 'dp'), may hold values from 0.1 to 3
- stale_grad: bfloat16 [16, 32768, 256], P('mp', 'dp'), may hold values from -6 to 6
- grad_owner: int32 [16, 32768, 1], P('mp', 'dp'), may hold values from 0 to 63; in each aligned block of 512 rows (0 to 511, 512 to 1023, ..., all dimensions but the last counted through in order) at most 16 rows name the same one
- grad_row: int32 [16, 32768], P('mp', 'dp'), may hold values from 0 to 511
- lookup_owner: int32 [16, 32768, 1], P('mp', 'dp'), may hold values from 0 to 63; in each aligned block of 512 rows (0 to 511, 512 to 1023, ..., all dimensions but the last counted through in order) at most 16 rows name the same one
- lookup_row: int32 [16, 32768], P('mp', 'dp'), may hold values from 0 to 511
- bag_len: int32 [16, 16384], P('mp', 'dp'), may hold values from 1 to 2
- label: int32 [16384], P('dp'), may hold values 0 or 1
- up_factor_weight: bfloat16 [2, 512, 4096], P(None, None, 'mp'), may hold values from -0.25 to 0.25
- v_weight: bfloat16 [2, 512, 4096], P(None, None, 'mp'), may hold values from -0.09375 to 0.09375
- cross_bias: float32 [2, 4096], P(None, 'mp'), may hold values from -3 to 3
- head_weight: float32 [4096], P('mp'), may hold values from -0.09375 to 0.09375
Outputs:
- new_table: float32 [16, 32768, 256], P('mp', 'dp')
- new_accum: float32 [16, 32768], P('mp', 'dp')
- grad_u: float32 [2, 512, 4096], P(None, 'dp', 'mp')
- grad_v: float32 [2, 512, 4096], P(None, 'dp', 'mp')
- grad_small: float32 [3, 4096], P(None, 'mp')
- grad_pooled: bfloat16 [16384, 4096], P('dp', 'mp')
Inputs may be any that keep to these rules, and one draw needn't show every extreme that they name: `grad_owner`: among the 512 blocks of one feature held by one index of dp, at most 16 name the same owner, and in some such group exactly 16 do. `lookup_owner`: among the 512 id slots of one feature belonging to one index of dp, at most 16 name the same owner, and in some such group exactly 16 do; slots k >= bag_len are unused.
All inputs are finite; a program needn't handle non-finite values. No bound on the sum of `label` on one device may be relied on, other than what follows from the above.
Results may differ from a plain program's by a relative error of at most 0.009.
Values may be sent and summed in bfloat16 or wider, within the bound.
No kernel may reach another device: no remote copies, remote signals or barrier semaphores. Data moves between devices by JAX's collectives and lax.ppermute only.
A program may use at most 128 MiB of HBM per device.

v0:
```python
import jax
import jax.numpy as jnp
from jax import lax
from jax.sharding import PartitionSpec as P

learn_rate = 0.5


def in_blocks(array, dim, devices):
    shape = array.shape
    parts = array.reshape(*shape[:dim], devices, shape[dim] // devices, *shape[dim + 1 :])
    return jnp.moveaxis(parts, dim, 0)


def sum_at_owner(array, axis, dim):
    parts = in_blocks(array, dim, lax.axis_size(axis))
    arrived = lax.all_to_all(parts, axis, split_axis=0, concat_axis=0, tiled=True)
    return arrived.sum(axis=0)


def copy_for_each(array, axis):
    copies = jnp.broadcast_to(array, (lax.axis_size(axis), *array.shape))
    return lax.all_to_all(copies, axis, split_axis=0, concat_axis=0, tiled=True)


def over_copies(array, axis):
    return copy_for_each(array, axis).sum(axis=0)


def side_by_side(arrays, axis, dim, along):
    widths = [a.shape[along] for a in arrays]
    both = jnp.concatenate(arrays, axis=along)
    filled = lax.psum_scatter(both, axis, scatter_dimension=dim, tiled=True)
    return tuple(jnp.split(filled, [sum(widths[:k]) for k in range(1, len(widths))], axis=along))


def bucket_slots(owners, capacity, peers):
    count = owners.shape[1]
    onehot = (owners[:, None, :] == jnp.arange(peers)[None, :, None]).astype(jnp.bfloat16)
    earlier = (jnp.arange(count)[:, None] < jnp.arange(count)[None, :]).astype(jnp.bfloat16)
    before = jnp.einsum("fpi,ij->fpj", onehot, earlier, preferred_element_type=jnp.float32)
    order_in = jnp.sum(before * onehot.astype(jnp.float32), axis=1)
    return owners * capacity + order_in.astype(jnp.int32)


def selection_matrix(indices, length):
    return (indices[:, :, None] == jnp.arange(length)[None, None, :]).astype(jnp.bfloat16)


def contract_last(left, right):
    return lax.dot_general(
        left, right, (((1,), (1,)), ((), ())), preferred_element_type=jnp.float32
    )


def contract_first(left, right):
    return lax.dot_general(
        left, right, (((0,), (0,)), ((), ())), preferred_element_type=jnp.float32
    )


def summed_rounded(partial, axis):
    share = lax.psum_scatter(partial, axis, scatter_dimension=0, tiled=True)
    return lax.all_gather(share.astype(jnp.bfloat16), axis, axis=0, tiled=True)


def cross_down(state, v_layer):
    return summed_rounded(contract_last(state, v_layer), "mp")


def local(
    embed_table,
    accum,
    stale_grad,
    grad_owner,
    grad_row,
    lookup_owner,
    lookup_row,
    bag_len,
    label,
    up_factor_weight,
    v_weight,
    cross_bias,
    head_weight,
):
    peers = lax.axis_size("dp")
    local_feats, grad_dev, width = stale_grad.shape
    rows_per_shard = embed_table.shape[1]
    which_feature = jnp.arange(local_feats)[:, None]
    grad_cap = max(2, 2 * grad_dev // peers)
    grad_total = peers * grad_cap
    grad_slot = bucket_slots(grad_owner[:, :, 0], grad_cap, peers)
    place = selection_matrix(grad_slot, grad_total)
    send_grads = jnp.einsum(
        "fns,fne->fse", place, stale_grad, preferred_element_type=jnp.float32
    ).astype(jnp.bfloat16)
    send_rows = (
        jnp.full((local_feats, grad_total), rows_per_shard, jnp.int32)
        .at[which_feature, grad_slot]
        .set(grad_row)
    )
    recv_grads = lax.all_to_all(
        send_grads.reshape(local_feats, peers, grad_cap, width),
        "dp",
        split_axis=1,
        concat_axis=1,
        tiled=True,
    )
    recv_rows = lax.all_to_all(
        send_rows.reshape(local_feats, peers, grad_cap),
        "dp",
        split_axis=1,
        concat_axis=1,
        tiled=True,
    )
    landing = selection_matrix(recv_rows.reshape(local_feats, grad_total), rows_per_shard)
    summed = jnp.einsum(
        "wjc,wjl->wcl",
        landing,
        recv_grads.reshape(local_feats, grad_total, width),
        preferred_element_type=jnp.float32,
    )
    new_accum = accum + jnp.mean(summed * summed, axis=2)
    new_table = embed_table - learn_rate * summed / jnp.sqrt(new_accum)[:, :, None]
    batch_dev = bag_len.shape[1]
    look_dev = lookup_row.shape[1]
    bag_size = look_dev // batch_dev
    look_cap = max(2, 2 * look_dev // peers)
    look_total = peers * look_cap
    look_slot = bucket_slots(lookup_owner[:, :, 0], look_cap, peers)
    wanted = (
        jnp.zeros((local_feats, look_total), jnp.int32).at[which_feature, look_slot].set(lookup_row)
    )
    requested_ids = lax.all_to_all(
        wanted.reshape(local_feats, peers, look_cap), "dp", split_axis=1, concat_axis=1, tiled=True
    ).reshape(local_feats, look_total)
    second_table = embed_table.astype(jnp.bfloat16)
    served = jnp.einsum(
        "adv,avm->adm",
        selection_matrix(requested_ids, rows_per_shard),
        second_table,
        preferred_element_type=jnp.float32,
    ).astype(jnp.bfloat16)
    returned = lax.all_to_all(
        served.reshape(local_feats, peers, look_cap, width),
        "dp",
        split_axis=1,
        concat_axis=1,
        tiled=True,
    ).reshape(local_feats, look_total, width)
    slots = look_slot.reshape(local_feats, batch_dev, bag_size)
    mixing = jnp.zeros((local_feats, batch_dev, look_total), jnp.bfloat16)
    for member in range(bag_size):
        used = (bag_len > member).astype(jnp.bfloat16)
        mixing = mixing + selection_matrix(slots[:, :, member], look_total) * used[:, :, None]
    pooled = jnp.einsum(
        "fbs,fse->fbe", mixing, returned, preferred_element_type=jnp.float32
    ).astype(jnp.bfloat16)
    start = jnp.transpose(pooled, (1, 0, 2)).reshape(batch_dev, local_feats * width)
    start_f = start.astype(jnp.float32)
    n_layers = up_factor_weight.shape[0]
    state = start
    states = []
    downs = []
    crosses = []
    for layer in range(n_layers):
        down_sum = cross_down(state, v_weight[layer])
        cross_out = (
            jnp.dot(down_sum, up_factor_weight[layer], preferred_element_type=jnp.float32)
            + cross_bias[layer]
        )
        states.append(state)
        downs.append(down_sum)
        crosses.append(cross_out)
        state = (start_f * cross_out + state.astype(jnp.float32)).astype(jnp.bfloat16)
    logit = lax.psum(jnp.sum(state.astype(jnp.float32) * head_weight[None, :], axis=1), "mp")
    slope = (jax.nn.sigmoid(logit) - label.astype(jnp.float32)) / jnp.sqrt(
        jnp.float32(batch_dev * peers)
    )
    upstream = slope[:, None] * head_weight[None, :]
    head_grad = jnp.sum(slope[:, None] * state.astype(jnp.float32), axis=0)
    to_start = jnp.zeros(start_f.shape, jnp.float32)
    grads_u = [None] * n_layers
    grads_v = [None] * n_layers
    bias_grads = [None] * n_layers
    for layer in reversed(range(n_layers)):
        direct = upstream * start_f
        bias_grads[layer] = jnp.sum(direct, axis=0)
        direct_bias_term = direct.astype(jnp.bfloat16)
        grad_u_layer = contract_first(downs[layer], direct_bias_term)
        back_sum = summed_rounded(contract_last(direct_bias_term, up_factor_weight[layer]), "mp")
        down_factor_gradient = contract_first(back_sum, states[layer])
        to_start = to_start + upstream * crosses[layer]
        upstream = upstream + jnp.dot(back_sum, v_weight[layer], preferred_element_type=jnp.float32)
        grads_u[layer] = grad_u_layer
        grads_v[layer] = down_factor_gradient
    grad_u = jnp.stack(grads_u)
    grad_v = jnp.stack(grads_v)
    grad_u, grad_v = side_by_side((grad_u, grad_v), "dp", 1, 0)
    grad_small = lax.psum(jnp.stack(bias_grads + [head_grad]), "dp")
    grad_pooled = (upstream + to_start).astype(jnp.bfloat16)
    return (new_table, new_accum, grad_u, grad_v, grad_small, grad_pooled)


def solution(mesh):
    return jax.shard_map(
        local,
        mesh=mesh,
        in_specs=(
            P("mp", "dp", None),
            P("mp", "dp"),
            P("mp", "dp", None),
            P("mp", "dp", None),
            P("mp", "dp"),
            P("mp", "dp", None),
            P("mp", "dp"),
            P("mp", "dp"),
            P("dp"),
            P(None, None, "mp"),
            P(None, None, "mp"),
            P(None, "mp"),
            P("mp"),
        ),
        out_specs=(
            P("mp", "dp", None),
            P("mp", "dp"),
            P(None, "dp", "mp"),
            P(None, "dp", "mp"),
            P(None, "mp"),
            P("dp", "mp"),
        ),
        check_vma=False,
    )
```

profile of v0, /device:TPU:0, one launch (start us, length us, event | category | flops | bytes accessed | tf_op | source)
XLA Modules:
  0.0 633.7 jit_solution(6955148603846393421)
XLA Ops:
  7.2 0.9 copy.63
  8.1 0.3 fusion.22
  8.5 0.7 broadcast_multiply_fusion
  9.2 0.7 copy.65
  9.9 0.3 fusion.21
  10.6 8.1 %scatter_custom_fusion.1 = s32[4096]{0:T(1024)S(1)} fusion(s32[2048]{0:T(1024)S(1)} %bitcast.111, s32[2048]{0:T(1024)S(1)} %bitcast.113, s32[]{:T(128)} %constant.5.clone.1), kind=kCustom, calls=%fused_computation.105 | custom fusion | bytes 16388
  18.9 21.1 %all_to_all.20 = s32[4,64,16]{2,0,1:T(4,128)S(1)} all-to-all(s32[4,64,16]{2,0,1:T(4,128)S(1)} %copy.43), channel_id=1, replica_groups=mesh['dp'=64,'mp'=4] {'dp'}, dimensions={1} | all-to-all | bytes 32768 | tf_op jit(solution)/shard_map/all_to_all | solution.py:134
  40.1 2.1 fusion.14
  42.1 1.6 copy.45
  43.8 4.7 all-to-all-start.3
  48.7 0.9 copy.39
  49.6 1.1 add.86
  50.6 0.2 fusion.78
  51.0 48.8 %all-to-all-done.3 = bf16[4,64,16,256]{3,2,0,1:T(8,128)(2,1)S(1)} async-done(((bf16[4,64,16,256]{3,2,0,1:T(8,128)(2,1)}), bf16[4,64,16,256]{3,2,0,1:T(8,128)(2,1)S(1)}, u32[]{:S(2)}, u32[]{:S(2)}) %all-to-all-start.3) | async-done | bytes 2097184 | tf_op jit(solution)/shard_map/all_to_all | solution.py:144
  99.8 0.2 copy.46
  100.0 2.1 fusion.17
  102.1 1.3 fusion.40
  103.5 0.2 copy.48
  103.7 20.2 %reduce-scatter.6.cloned.1.call-done = f32[64,512]{1,0:T(8,128)} async-done(((f32[256,512]{1,0:T(8,128)}), f32[64,512]{1,0:T(8,128)}) %reduce-scatter.6.cloned.1.call-update) | async-done | bytes 131088 | tf_op jit(solution)/shard_map/reduce_scatter | solution.py:63
  123.9 1.1 convert_element_type.138
  125.0 12.3 %all_gather.12 = bf16[256,512]{1,0:T(8,128)(2,1)S(1)} all-gather(bf16[64,512]{1,0:T(8,128)(2,1)S(1)} %convert_element_type.138), channel_id=1, replica_groups=mesh['dp'=64,'mp'=4] {'mp'}, dimensions={0}, use_global_device_ids=true | all-gather | bytes 327680 | tf_op jit(solution)/shard_map/all_gather | solution.py:64
  137.3 2.8 fusion.26
  140.1 1.3 fusion.34
  141.5 23.9 %reduce-scatter.8.cloned.1.call-done = f32[64,512]{1,0:T(8,128)} async-done(((f32[256,512]{1,0:T(8,128)}), f32[64,512]{1,0:T(8,128)}) %reduce-scatter.8.cloned.1.call-update) | async-done | bytes 131088 | tf_op jit(solution)/shard_map/reduce_scatter | solution.py:63
  165.3 0.9 convert_element_type.141
  166.3 12.3 %all_gather.13 = bf16[256,512]{1,0:T(8,128)(2,1)S(1)} all-gather(bf16[64,512]{1,0:T(8,128)(2,1)S(1)} %convert_element_type.141), channel_id=1, replica_groups=mesh['dp'=64,'mp'=4] {'mp'}, dimensions={0}, use_global_device_ids=true | all-gather | bytes 327680 | tf_op jit(solution)/shard_map/all_gather | solution.py:64
  178.5 2.9 fusion.23
  181.4 8.4 %psum.14 = f32[256]{0:T(256)S(1)} all-reduce(f32[256]{0:T(256)S(1)} %get-tuple-element.28), channel_id=1, replica_groups=mesh['dp'=64,'mp'=4] {'mp'}, use_global_device_ids=true, to_apply=%region_8.0 | all-reduce | flops 256 | bytes 2048 | tf_op jit(solution)/shard_map/psum | solution.py:176
  189.8 0.4 fusion.42
  190.2 2.5 fusion.30
  192.8 23.7 %reduce-scatter.10.cloned.1.call-done = f32[64,512]{1,0:T(8,128)} async-done(((f32[256,512]{1,0:T(8,128)}), f32[64,512]{1,0:T(8,128)}) %reduce-scatter.10.cloned.1.call-update) | async-done | bytes 131088 | tf_op jit(solution)/shard_map/reduce_scatter | solution.py:63
  216.5 1.1 convert_element_type.149
  217.5 12.3 %all_gather.14 = bf16[256,512]{1,0:T(8,128)(2,1)S(1)} all-gather(bf16[64,512]{1,0:T(8,128)(2,1)S(1)} %convert_element_type.149), channel_id=1, replica_groups=mesh['dp'=64,'mp'=4] {'mp'}, dimensions={0}, use_global_device_ids=true | all-gather | bytes 327680 | tf_op jit(solution)/shard_map/all_gather | solution.py:64
  229.8 0.7 copy-done.10
  230.5 1.7 fusion.59
  232.2 1.3 fusion.36
  233.5 0.2 reduce-scatter.14.cloned.1.call-start
  233.8 1.9 convolution_bitcast_fusion.2
  235.7 1.8 convolution_bitcast_fusion
  237.5 1.8 convolution_bitcast_fusion.3
  239.3 18.1 %reduce-scatter.12.cloned.1.call-done = f32[64,512]{1,0:T(8,128)} async-done(((f32[256,512]{1,0:T(8,128)}), f32[64,512]{1,0:T(8,128)}) %reduce-scatter.12.cloned.1.call-update) | async-done | bytes 131088 | tf_op jit(solution)/shard_map/reduce_scatter | solution.py:63
  257.4 1.1 convert_element_type.152
  258.5 12.3 %all_gather.15 = bf16[256,512]{1,0:T(8,128)(2,1)S(1)} all-gather(bf16[64,512]{1,0:T(8,128)(2,1)S(1)} %convert_element_type.152), channel_id=1, replica_groups=mesh['dp'=64,'mp'=4] {'mp'}, dimensions={0}, use_global_device_ids=true | all-gather | bytes 327680 | tf_op jit(solution)/shard_map/all_gather | solution.py:64
  270.7 0.5 convolution_bitcast_fusion.1
  271.2 5.2 pad_maximum_fusion
  276.5 0.7 copy-done.18
  277.1 8.1 %scatter_custom_fusion = s32[4096]{0:T(1024)S(1)} fusion(s32[2048]{0:T(1024)S(1)} %bitcast.112, s32[2048]{0:T(1024)S(1)} %bitcast.114, s32[]{:T(128)} %constant.11.clone.1), kind=kCustom, calls=%fused_computation.107 | custom fusion | bytes 16388
  285.3 0.7 copy.33
  286.0 10.4 %all-to-all-start = ((s32[4,64,16]{2,0,1:T(4,128)}), s32[4,64,16]{2,0,1:T(4,128)S(1)}, u32[]{:S(2)}, u32[]{:S(2)}) async-start(s32[4,64,16]{2,0,1:T(4,128)} %copy.33), calls=%async_computation | async-start | bytes 262144 | tf_op jit(solution)/shard_map/all_to_all | solution.py:109
  296.5 1.5 fusion.15
  298.0 1.6 copy.35
  299.6 7.9 %all-to-all-done = s32[4,64,16]{2,0,1:T(4,128)S(1)} async-done(((s32[4,64,16]{2,0,1:T(4,128)}), s32[4,64,16]{2,0,1:T(4,128)S(1)}, u32[]{:S(2)}, u32[]{:S(2)}) %all-to-all-start) | async-done | bytes 16416 | tf_op jit(solution)/shard_map/all_to_all | solution.py:109
  307.5 5.6 all-to-all-start.1
  313.1 2.9 copy.38
  316.2 49.0 %all-to-all-done.1 = bf16[4,64,16,256]{3,2,0,1:T(8,128)(2,1)} async-done(((bf16[4,64,16,256]{3,2,0,1:T(8,128)(2,1)}), bf16[4,64,16,256]{3,2,0,1:T(8,128)(2,1)}, u32[]{:S(2)}, u32[]{:S(2)}) %all-to-all-start.1) | async-done | bytes 2097184 | tf_op jit(solution)/shard_map/all_to_all | solution.py:102
  365.1 1.8 copy.36
  367.0 2.9 multiply_reduce_fusion
  369.9 0.6 fusion.77
  370.5 1.9 divide_subtract_fusion
  372.4 3.0 copy.49
  375.4 1.2 fusion.24
  376.6 246.2 %psum.15 = f32[3,1024]{1,0:T(4,128)} all-reduce(f32[3,1024]{1,0:T(4,128)S(1)} %pad_maximum_fusion.1), channel_id=1, replica_groups=mesh['dp'=64,'mp'=4] {'dp'}, use_global_device_ids=true, to_apply=%region_15.0 | all-reduce | flops 3072 | bytes 24576 | tf_op jit(solution)/shard_map/psum | solution.py:200
  622.8 2.8 fusion.20
  625.6 1.5 fusion.79
  (84 shorter events, 1.6 us)
Async XLA Ops:
  7.2 289.3 %copy-start = (bf16[4,512,256]{2,1,0:T(8,128)(2,1)S(1)}, bf16[4,512,256]{2,1,0:T(8,128)(2,1)}, u32[]{:S(2)}) copy-start(bf16[4,512,256]{2,1,0:T(8,128)(2,1)} %param.15) | copy-start | bytes 3145732
  7.2 3.1 copy-start.23
  7.2 3.2 copy-start.22
  7.2 3.0 copy-start.15
  7.2 3.4 copy-start.16
  7.2 32.8 %copy-start.9 = (f32[4,512,256]{2,1,0:T(8,128)S(1)}, f32[4,512,256]{2,1,0:T(8,128)}, u32[]{:S(2)}) copy-start(f32[4,512,256]{2,1,0:T(8,128)} %param.13) | copy-start | bytes 6291460
  43.8 56.1 %all-to-all-start.3 = ((bf16[4,64,16,256]{3,2,0,1:T(8,128)(2,1)}), bf16[4,64,16,256]{3,2,0,1:T(8,128)(2,1)S(1)}, u32[]{:S(2)}, u32[]{:S(2)}) async-start(bf16[4,64,16,256]{3,2,0,1:T(8,128)(2,1)} %copy.45), calls=%async_computation.3 | async-start | bytes 4194304 | tf_op jit(solution)/shard_map/all_to_all | solution.py:144
  48.5 2.5 copy-start.20
  48.5 75.4 %reduce-scatter.6.cloned.1.call-start = ((), (), s32[]{:S(2)}) async-start(), calls=%async_computation.9 | async-start | bytes 655360 | tf_op jit(solution)/shard_map/reduce_scatter | solution.py:63
  100.0 2.1 copy-start.12
  102.1 1.4 copy-start.17
  103.4 61.9 %reduce-scatter.8.cloned.1.call-start = ((), (), s32[]{:S(2)}) async-start(), calls=%async_computation.10 | async-start | bytes 655360 | tf_op jit(solution)/shard_map/reduce_scatter | solution.py:63
  123.9 16.2 %copy-start.13 = (bf16[2,512,1024]{2,1,0:T(8,128)(2,1)S(1)}, bf16[2,512,1024]{2,1,0:T(8,128)(2,1)}, u32[]{:S(2)}) copy-start(bf16[2,512,1024]{2,1,0:T(8,128)(2,1)} %param.23) | copy-start | bytes 6291460
  137.3 4.1 copy-start.7
  140.1 41.3 %copy-start.4 = (bf16[256,1024]{1,0:T(8,128)(2,1)}, bf16[256,1024]{1,0:T(8,128)(2,1)S(1)}, u32[]{:S(2)}) copy-start(bf16[256,1024]{1,0:T(8,128)(2,1)S(1)} %get-tuple-element.48) | copy-start | bytes 1572868
  140.1 1.4 copy-start.14
  141.4 75.1 %reduce-scatter.10.cloned.1.call-start = ((), (), s32[]{:S(2)}) async-start(), calls=%async_computation.11 | async-start | bytes 655360 | tf_op jit(solution)/shard_map/reduce_scatter | solution.py:63
  166.2 23.5 %copy-start.21 = (s32[256]{0:T(256)S(1)}, s32[256]{0:T(256)}, u32[]{:S(2)}) copy-start(s32[256]{0:T(256)} %param.21) | copy-start | bytes 3076
  192.7 64.7 %reduce-scatter.12.cloned.1.call-start = ((), (), s32[]{:S(2)}) async-start(), calls=%async_computation.12 | async-start | bytes 655360 | tf_op jit(solution)/shard_map/reduce_scatter | solution.py:63
  216.5 15.7 %copy-start.3 = (bf16[2,512,1024]{2,1,0:T(8,128)(2,1)S(1)}, bf16[2,512,1024]{2,1,0:T(8,128)(2,1)}, u32[]{:S(2)}) copy-start(bf16[2,512,1024]{2,1,0:T(8,128)(2,1)} %param.22) | copy-start | bytes 6291460
  229.8 0.7 copy-start.10
  233.5 392.1 %reduce-scatter.14.cloned.1.call-start = ((), (), s32[]{:S(2)}) async-start(), calls=%async_computation.13 | async-start | bytes 8519680 | tf_op jit(solution)/shard_map/reduce_scatter | solution.py:33
  233.8 1.9 copy-start.5
  233.8 1.9 copy-start.11
  235.7 1.8 copy-start.8
  257.4 13.8 %copy-start.2 = (f32[1,512,1024]{2,1,0:T(8,128)S(1)}, f32[1,512,1024]{2,1,0:T(8,128)}, u32[]{:S(2)}) copy-start(f32[1,512,1024]{2,1,0:T(8,128)} %convolution_bitcast_fusion.2) | copy-start | bytes 6291460
  276.4 0.7 copy-start.18
  286.0 21.5 %all-to-all-start = ((s32[4,64,16]{2,0,1:T(4,128)}), s32[4,64,16]{2,0,1:T(4,128)S(1)}, u32[]{:S(2)}, u32[]{:S(2)}) async-start(s32[4,64,16]{2,0,1:T(4,128)} %copy.33), calls=%async_computation | async-start | bytes 262144 | tf_op jit(solution)/shard_map/all_to_all | solution.py:109
  307.5 57.6 %all-to-all-start.1 = ((bf16[4,64,16,256]{3,2,0,1:T(8,128)(2,1)}), bf16[4,64,16,256]{3,2,0,1:T(8,128)(2,1)}, u32[]{:S(2)}, u32[]{:S(2)}) async-start(bf16[4,64,16,256]{3,2,0,1:T(8,128)(2,1)} %copy.35), calls=%async_computation.1 | async-start | bytes 4194304 | tf_op jit(solution)/shard_map/all_to_all | solution.py:102
  366.9 2.9 copy-start.19
  367.0 3.5 copy-start.1
  372.4 250.5 %copy-start.6 = (f32[256,1024]{1,0:T(8,128)S(1)}, f32[256,1024]{1,0:T(8,128)}, u32[]{:S(2)}) copy-start(f32[256,1024]{1,0:T(8,128)} %get-tuple-element.50) | copy-start | bytes 3145732
Sparse Core Ops, SparseCore 0:
  103.5 20.3 reduce-scatter.5
  141.5 23.7 reduce-scatter.7
  192.8 23.5 reduce-scatter.9
  233.7 23.7 reduce-scatter.11
  276.6 150.7 reduce-scatter.13
where the time goes:
time: 635 us; the launch traced here: 634 us
  blocking collectives  325 us (51%)
  waiting for transfers between devices  192 us (30%)
  local copies, waits for them, and re-layouts  34.7 us (5%)
  matrix products  31.7 us (5%)
  starting transfers between devices  21.1 us (3%)
  other arithmetic  15.5 us (2%)
  between operations  14.3 us (2%)
    psum x1, blocking collectives, local(): grad_small = lax.psum(jnp.stack(bias_grads + [head_grad]), 'dp')  246 us
    reduce_scatter x4, waiting for transfers between devices, summed_rounded(): share = lax.psum_scatter(partial, axis, scatter_dimension=0, tiled=True)  85.9 us
    all_gather x4, blocking collectives, summed_rounded(): return lax.all_gather(share.astype(jnp.bfloat16), axis, axis=0, tiled=True)  49 us
    all_to_all x1, waiting for transfers between devices, local(): lax.all_to_all(send_grads.reshape(local_feats, peers, grad_cap, width), '...  49 us
    all_to_all x1, waiting for transfers between devices, local(): lax.all_to_all(served.reshape(local_feats, peers, look_cap, width), 'dp',...  48.8 us
    unnamed x60, local copies, waits for them, and re-layouts  25.1 us
    all_to_all x1, blocking collectives, local(): lax.all_to_all(wanted.reshape(local_feats, peers, look_cap), 'dp', split_...  21.1 us
  transfers between devices with their start and end apart: 8, of which 7 were waited for; matrix products, arithmetic and copies ran while one was open for 6% of the time, Pallas kernels for 0%

commit v1 on v0

--- a/solution.py
+++ b/solution.py
@@ -106,12 +106,18 @@
         concat_axis=1,
         tiled=True,
     )
-    recv_rows = lax.all_to_all(
-        send_rows.reshape(local_feats, peers, grad_cap),
-        "dp",
-        split_axis=1,
-        concat_axis=1,
-        tiled=True,
+    recv_rows = jnp.concatenate(
+        lax.all_to_all(
+            jnp.stack(
+                jnp.split(
+                    send_rows.reshape(local_feats, peers, grad_cap), lax.axis_size("dp"), axis=1
+                )
+            ),
+            "dp",
+            0,
+            0,
+        ),
+        axis=1,
     )
     landing = selection_matrix(recv_rows.reshape(local_feats, grad_total), rows_per_shard)
     summed = jnp.einsum(

time: 635 us -> 670 us (1.055)
  local copies, waits for them, and re-layouts: 34.7 us -> 71 us
    unnamed x60 -> x159, local copies, waits for them, and re-layouts: 25.1 us -> 60.7 us
    reduce_scatter x4, waiting for transfers between devices: 85.9 us -> 71.5 us  [summed_rounded(): share = lax.psum_scatter(partial, axis, scatter_dimension=0, tiled=True)]
    all_to_all x1, waiting for transfers between devices: 49 us -> 58.5 us  [local(): lax.all_to_all(send_grads.reshape(local_feats, peers, grad_cap, width), '...]
  transfers between devices with their start and end apart: 8 -> 8, of which waited for: 7 -> 7; matrix products, arithmetic and copies ran while one was open for 6% -> 11% of each run, Pallas kernels for 0% -> 0%
where the time goes in v1:
time: 670 us; the launch traced here: 667 us
  blocking collectives  326 us (49%)
  waiting for transfers between devices  187 us (28%)
  local copies, waits for them, and re-layouts  71 us (11%)
  matrix products  32.4 us (5%)
  starting transfers between devices  20.9 us (3%)
  other arithmetic  16.2 us (2%)
  between operations  14.5 us (2%)
    psum x1, blocking collectives, local(): grad_small = lax.psum(jnp.stack(bias_grads + [head_grad]), 'dp')  247 us
    reduce_scatter x4, waiting for transfers between devices, summed_rounded(): share = lax.psum_scatter(partial, axis, scatter_dimension=0, tiled=True)  71.5 us
    unnamed x159, local copies, waits for them, and re-layouts  60.7 us
    all_to_all x1, waiting for transfers between devices, local(): lax.all_to_all(send_grads.reshape(local_feats, peers, grad_cap, width), '...  58.5 us
    all_gather x4, blocking collectives, summed_rounded(): return lax.all_gather(share.astype(jnp.bfloat16), axis, axis=0, tiled=True)  49.2 us
    all_to_all x1, waiting for transfers between devices, local(): lax.all_to_all(served.reshape(local_feats, peers, look_cap, width), 'dp',...  48.8 us
    all_to_all x1, blocking collectives, local(): lax.all_to_all(wanted.reshape(local_feats, peers, look_cap), 'dp', split_...  21.1 us
  transfers between devices with their start and end apart: 8, of which 7 were waited for; matrix products, arithmetic and copies ran while one was open for 11% of the time, Pallas kernels for 0%

profile of v1, /device:TPU:0, one launch (start us, length us, event | category | flops | bytes accessed | tf_op | source)
XLA Modules:
  0.0 667.5 jit_solution(11305859581277381816)
XLA Ops:
  7.2 0.9 copy.225
  8.5 0.7 broadcast_multiply_fusion
  9.2 0.7 copy.227
  10.6 8.1 %scatter_custom_fusion.1 = s32[4096]{0:T(1024)S(1)} fusion(s32[2048]{0:T(1024)S(1)} %bitcast.246, s32[2048]{0:T(1024)S(1)} %bitcast.248, s32[]{:T(128)} %constant.5.clone.1), kind=kCustom, calls=%fused_computation.169 | custom fusion | bytes 16388
  18.9 21.1 %all_to_all.20 = s32[4,64,16]{2,0,1:T(4,128)S(1)} all-to-all(s32[4,64,16]{2,0,1:T(4,128)S(1)} %copy.205), channel_id=1, replica_groups=mesh['dp'=64,'mp'=4] {'dp'}, dimensions={1} | all-to-all | bytes 32768 | tf_op jit(solution)/shard_map/all_to_all | solution.py:140
  40.1 2.1 fusion.14
  42.1 1.6 copy.207
  43.8 4.7 all-to-all-start.3
  48.7 0.9 copy.201
  49.6 1.1 add.86
  51.0 48.8 %all-to-all-done.3 = bf16[4,64,16,256]{3,2,0,1:T(8,128)(2,1)S(1)} async-done(((bf16[4,64,16,256]{3,2,0,1:T(8,128)(2,1)}), bf16[4,64,16,256]{3,2,0,1:T(8,128)(2,1)S(1)}, u32[]{:S(2)}, u32[]{:S(2)}) %all-to-all-start.3) | async-done | bytes 2097184 | tf_op jit(solution)/shard_map/all_to_all | solution.py:150
  100.0 2.1 fusion.17
  102.1 1.3 fusion.40
  103.7 20.2 %reduce-scatter.6.cloned.1.call-done = f32[64,512]{1,0:T(8,128)} async-done(((f32[256,512]{1,0:T(8,128)}), f32[64,512]{1,0:T(8,128)}) %reduce-scatter.6.cloned.1.call-update) | async-done | bytes 131088 | tf_op jit(solution)/shard_map/reduce_scatter | solution.py:63
  123.9 1.1 convert_element_type.138
  125.0 12.3 %all_gather.12 = bf16[256,512]{1,0:T(8,128)(2,1)S(1)} all-gather(bf16[64,512]{1,0:T(8,128)(2,1)S(1)} %convert_element_type.138), channel_id=1, replica_groups=mesh['dp'=64,'mp'=4] {'mp'}, dimensions={0}, use_global_device_ids=true | all-gather | bytes 327680 | tf_op jit(solution)/shard_map/all_gather | solution.py:64
  137.3 2.8 fusion.26
  140.1 1.3 fusion.34
  141.5 23.8 %reduce-scatter.8.cloned.1.call-done = f32[64,512]{1,0:T(8,128)} async-done(((f32[256,512]{1,0:T(8,128)}), f32[64,512]{1,0:T(8,128)}) %reduce-scatter.8.cloned.1.call-update) | async-done | bytes 131088 | tf_op jit(solution)/shard_map/reduce_scatter | solution.py:63
  165.3 0.9 convert_element_type.141
  166.2 12.3 %all_gather.13 = bf16[256,512]{1,0:T(8,128)(2,1)S(1)} all-gather(bf16[64,512]{1,0:T(8,128)(2,1)S(1)} %convert_element_type.141), channel_id=1, replica_groups=mesh['dp'=64,'mp'=4] {'mp'}, dimensions={0}, use_global_device_ids=true | all-gather | bytes 327680 | tf_op jit(solution)/shard_map/all_gather | solution.py:64
  178.5 2.9 fusion.23
  181.3 8.4 %psum.14 = f32[256]{0:T(256)S(1)} all-reduce(f32[256]{0:T(256)S(1)} %get-tuple-element.40), channel_id=1, replica_groups=mesh['dp'=64,'mp'=4] {'mp'}, use_global_device_ids=true, to_apply=%region_8.0 | all-reduce | flops 256 | bytes 2048 | tf_op jit(solution)/shard_map/psum | solution.py:182
  189.8 1.0 fusion.42
  190.8 2.5 fusion.30
  193.4 8.1 %scatter_custom_fusion = s32[4096]{0:T(1024)S(1)} fusion(s32[2048]{0:T(1024)S(1)} %bitcast.247, s32[2048]{0:T(1024)S(1)} %bitcast.249, s32[]{:T(128)} %constant.11.clone.1), kind=kCustom, calls=%fused_computation.171 | custom fusion | bytes 16388
  201.6 0.6 constant_dynamic-update-slice_fusion.63
  205.6 11.5 %reduce-scatter.10.cloned.1.call-done = f32[64,512]{1,0:T(8,128)} async-done(((f32[256,512]{1,0:T(8,128)}), f32[64,512]{1,0:T(8,128)}) %reduce-scatter.10.cloned.1.call-update) | async-done | bytes 131088 | tf_op jit(solution)/shard_map/reduce_scatter | solution.py:63
  217.1 1.1 convert_element_type.149
  218.2 12.4 %all_gather.14 = bf16[256,512]{1,0:T(8,128)(2,1)S(1)} all-gather(bf16[64,512]{1,0:T(8,128)(2,1)S(1)} %convert_element_type.149), channel_id=1, replica_groups=mesh['dp'=64,'mp'=4] {'mp'}, dimensions={0}, use_global_device_ids=true | all-gather | bytes 327680 | tf_op jit(solution)/shard_map/all_gather | solution.py:64
  230.6 0.7 copy-done.10
  231.3 2.3 fusion.59
  233.6 1.3 fusion.36
  235.0 0.7 fusion.82
  237.4 1.9 convolution_bitcast_fusion.2
  239.2 1.8 convolution_bitcast_fusion
  241.0 1.9 convolution_bitcast_fusion.3
  242.9 15.9 %reduce-scatter.12.cloned.1.call-done = f32[64,512]{1,0:T(8,128)} async-done(((f32[256,512]{1,0:T(8,128)}), f32[64,512]{1,0:T(8,128)}) %reduce-scatter.12.cloned.1.call-update) | async-done | bytes 131088 | tf_op jit(solution)/shard_map/reduce_scatter | solution.py:63
  258.8 1.1 convert_element_type.152
  259.9 12.3 %all_gather.15 = bf16[256,512]{1,0:T(8,128)(2,1)S(1)} all-gather(bf16[64,512]{1,0:T(8,128)(2,1)S(1)} %convert_element_type.152), channel_id=1, replica_groups=mesh['dp'=64,'mp'=4] {'mp'}, dimensions={0}, use_global_device_ids=true | all-gather | bytes 327680 | tf_op jit(solution)/shard_map/all_gather | solution.py:64
  272.6 5.3 pad_maximum_fusion
  280.9 0.6 constant_dynamic-update-slice_fusion.49
  283.7 0.6 constant_dynamic-update-slice_fusion.44
  293.4 0.6 constant_dynamic-update-slice_fusion.27
  303.0 0.6 constant_dynamic-update-slice_fusion.10
  304.2 0.6 constant_dynamic-update-slice_fusion.8
  307.7 0.6 constant_dynamic-update-slice_fusion.2
  308.8 0.6 constant_dynamic-update-slice_fusion
  309.4 10.4 %all-to-all-start = ((s32[64,4,1,16]{3,2,1,0:T(1,128)}), s32[64,4,1,16]{3,2,1,0:T(1,128)S(1)}, u32[]{:S(2)}, u32[]{:S(2)}) async-start(s32[64,4,1,16]{3,2,1,0:T(1,128)} %bitcast.65), calls=%async_computation | async-start | bytes 262144 | tf_op jit(solution)/shard_map/all_to_all | solution.py:110
  319.9 1.5 fusion.15
  321.3 1.7 copy.197
  323.0 7.8 %all-to-all-done = s32[64,4,1,16]{3,2,1,0:T(1,128)S(1)} async-done(((s32[64,4,1,16]{3,2,1,0:T(1,128)}), s32[64,4,1,16]{3,2,1,0:T(1,128)S(1)}, u32[]{:S(2)}, u32[]{:S(2)}) %all-to-all-start) | async-done | bytes 16416 | tf_op jit(solution)/shard_map/all_to_all | solution.py:110
  330.8 5.6 all-to-all-start.1
  336.4 2.9 copy.200
  339.5 58.5 %all-to-all-done.1 = bf16[4,64,16,256]{3,2,0,1:T(8,128)(2,1)} async-done(((bf16[4,64,16,256]{3,2,0,1:T(8,128)(2,1)}), bf16[4,64,16,256]{3,2,0,1:T(8,128)(2,1)}, u32[]{:S(2)}, u32[]{:S(2)}) %all-to-all-start.1) | async-done | bytes 2097184 | tf_op jit(solution)/shard_map/all_to_all | solution.py:102
  398.0 1.8 copy.198
  399.8 2.9 multiply_reduce_fusion
  402.7 0.6 fusion.77
  403.3 1.9 divide_subtract_fusion
  405.2 3.0 copy.211
  408.2 1.2 fusion.24
  409.5 247.1 %psum.15 = f32[3,1024]{1,0:T(4,128)} all-reduce(f32[3,1024]{1,0:T(4,128)S(1)} %pad_maximum_fusion.1), channel_id=1, replica_groups=mesh['dp'=64,'mp'=4] {'dp'}, use_global_device_ids=true, to_apply=%region_15.0 | all-reduce | flops 3072 | bytes 24576 | tf_op jit(solution)/shard_map/psum | solution.py:206
  656.6 2.8 fusion.20
  659.4 1.5 fusion.79
  (187 shorter events, 35.6 us)
Async XLA Ops:
  7.2 312.7 %copy-start = (bf16[4,512,256]{2,1,0:T(8,128)(2,1)S(1)}, bf16[4,512,256]{2,1,0:T(8,128)(2,1)}, u32[]{:S(2)}) copy-start(bf16[4,512,256]{2,1,0:T(8,128)(2,1)} %param.15) | copy-start | bytes 3145732
  7.2 3.1 copy-start.41
  7.2 3.2 copy-start.40
  7.2 3.0 copy-start.15
  7.2 3.4 copy-start.33
  7.2 32.8 %copy-start.9 = (f32[4,512,256]{2,1,0:T(8,128)S(1)}, f32[4,512,256]{2,1,0:T(8,128)}, u32[]{:S(2)}) copy-start(f32[4,512,256]{2,1,0:T(8,128)} %param.13) | copy-start | bytes 6291460
  43.8 56.1 %all-to-all-start.3 = ((bf16[4,64,16,256]{3,2,0,1:T(8,128)(2,1)}), bf16[4,64,16,256]{3,2,0,1:T(8,128)(2,1)S(1)}, u32[]{:S(2)}, u32[]{:S(2)}) async-start(bf16[4,64,16,256]{3,2,0,1:T(8,128)(2,1)} %copy.207), calls=%async_computation.3 | async-start | bytes 4194304 | tf_op jit(solution)/shard_map/all_to_all | solution.py:150
  48.5 2.5 copy-start.38
  48.5 75.4 %reduce-scatter.6.cloned.1.call-start = ((), (), s32[]{:S(2)}) async-start(), calls=%async_computation.9 | async-start | bytes 655360 | tf_op jit(solution)/shard_map/reduce_scatter | solution.py:63
  100.0 2.1 copy-start.12
  102.1 1.4 copy-start.34
  103.4 61.9 %reduce-scatter.8.cloned.1.call-start = ((), (), s32[]{:S(2)}) async-start(), calls=%async_computation.10 | async-start | bytes 655360 | tf_op jit(solution)/shard_map/reduce_scatter | solution.py:63
  123.9 16.2 %copy-start.13 = (bf16[2,512,1024]{2,1,0:T(8,128)(2,1)S(1)}, bf16[2,512,1024]{2,1,0:T(8,128)(2,1)}, u32[]{:S(2)}) copy-start(bf16[2,512,1024]{2,1,0:T(8,128)(2,1)} %param.23) | copy-start | bytes 6291460
  137.3 4.1 copy-start.7
  140.1 41.2 %copy-start.4 = (bf16[256,1024]{1,0:T(8,128)(2,1)}, bf16[256,1024]{1,0:T(8,128)(2,1)S(1)}, u32[]{:S(2)}) copy-start(bf16[256,1024]{1,0:T(8,128)(2,1)S(1)} %get-tuple-element.124) | copy-start | bytes 1572868
  140.1 1.4 copy-start.14
  141.4 75.7 %reduce-scatter.10.cloned.1.call-start = ((), (), s32[]{:S(2)}) async-start(), calls=%async_computation.11 | async-start | bytes 655360 | tf_op jit(solution)/shard_map/reduce_scatter | solution.py:63
  166.2 23.6 %copy-start.39 = (s32[256]{0:T(256)S(1)}, s32[256]{0:T(256)}, u32[]{:S(2)}) copy-start(s32[256]{0:T(256)} %param.21) | copy-start | bytes 3076
  181.3 12.0 %copy-start.35 = (s32[4,512]{1,0:T(4,128)S(1)}, s32[4,512]{1,0:T(4,128)}, u32[]{:S(2)}) copy-start(s32[4,512]{1,0:T(4,128)} %param.17) | copy-start | bytes 24580
  193.3 65.5 %reduce-scatter.12.cloned.1.call-start = ((), (), s32[]{:S(2)}) async-start(), calls=%async_computation.12 | async-start | bytes 655360 | tf_op jit(solution)/shard_map/reduce_scatter | solution.py:63
  217.1 16.5 %copy-start.3 = (bf16[2,512,1024]{2,1,0:T(8,128)(2,1)S(1)}, bf16[2,512,1024]{2,1,0:T(8,128)(2,1)}, u32[]{:S(2)}) copy-start(bf16[2,512,1024]{2,1,0:T(8,128)(2,1)} %param.22) | copy-start | bytes 6291460
  230.6 0.7 copy-start.10
  234.9 424.5 %reduce-scatter.14.cloned.1.call-start = ((), (), s32[]{:S(2)}) async-start(), calls=%async_computation.13 | async-start | bytes 8519680 | tf_op jit(solution)/shard_map/reduce_scatter | solution.py:33
  235.0 4.3 copy-start.5
  235.0 4.3 copy-start.11
  239.2 1.8 copy-start.8
  258.8 13.8 %copy-start.2 = (f32[1,512,1024]{2,1,0:T(8,128)S(1)}, f32[1,512,1024]{2,1,0:T(8,128)}, u32[]{:S(2)}) copy-start(f32[1,512,1024]{2,1,0:T(8,128)} %convolution_bitcast_fusion.2) | copy-start | bytes 6291460
  277.9 0.7 copy-start.32
  277.9 1.2 copy-start.31
  277.9 1.8 copy-start.30
  277.9 2.4 copy-start.29
  277.9 2.9 copy-start.28
  278.0 3.5 copy-start.27
  278.0 4.1 copy-start.26
  278.0 4.6 copy-start.25
  278.0 5.2 copy-start.24
  278.0 5.7 copy-start.23
  278.0 6.3 copy-start.22
  278.0 6.9 %copy-start.21 = (s32[4,1,16]{2,1,0:T(1,128)S(1)}, s32[4,1,16]{2,1,0:T(1,128)}, u32[]{:S(2)}) copy-start(s32[4,1,16]{2,1,0:T(1,128)} %get-tuple-element.94) | copy-start | bytes 772
  278.0 7.4 %copy-start.20 = (s32[4,1,16]{2,1,0:T(1,128)S(1)}, s32[4,1,16]{2,1,0:T(1,128)}, u32[]{:S(2)}) copy-start(s32[4,1,16]{2,1,0:T(1,128)} %get-tuple-element.93) | copy-start | bytes 772
  278.0 8.0 %copy-start.19 = (s32[4,1,16]{2,1,0:T(1,128)S(1)}, s32[4,1,16]{2,1,0:T(1,128)}, u32[]{:S(2)}) copy-start(s32[4,1,16]{2,1,0:T(1,128)} %get-tuple-element.92) | copy-start | bytes 772
  278.0 8.5 %copy-start.18 = (s32[4,1,16]{2,1,0:T(1,128)S(1)}, s32[4,1,16]{2,1,0:T(1,128)}, u32[]{:S(2)}) copy-start(s32[4,1,16]{2,1,0:T(1,128)} %get-tuple-element.91) | copy-start | bytes 772
  278.1 9.1 %copy-start.17 = (s32[4,1,16]{2,1,0:T(1,128)S(1)}, s32[4,1,16]{2,1,0:T(1,128)}, u32[]{:S(2)}) copy-start(s32[4,1,16]{2,1,0:T(1,128)} %get-tuple-element.90) | copy-start | bytes 772
  309.4 21.5 %all-to-all-start = ((s32[64,4,1,16]{3,2,1,0:T(1,128)}), s32[64,4,1,16]{3,2,1,0:T(1,128)S(1)}, u32[]{:S(2)}, u32[]{:S(2)}) async-start(s32[64,4,1,16]{3,2,1,0:T(1,128)} %bitcast.65), calls=%async_computation | async-start | bytes 262144 | tf_op jit(solution)/shard_map/all_to_all | solution.py:110
  330.8 67.2 %all-to-all-start.1 = ((bf16[4,64,16,256]{3,2,0,1:T(8,128)(2,1)}), bf16[4,64,16,256]{3,2,0,1:T(8,128)(2,1)}, u32[]{:S(2)}, u32[]{:S(2)}) async-start(bf16[4,64,16,256]{3,2,0,1:T(8,128)(2,1)} %copy.197), calls=%async_computation.1 | async-start | bytes 4194304 | tf_op jit(solution)/shard_map/all_to_all | solution.py:102
  399.8 2.9 copy-start.36
  399.8 3.5 copy-start.1
  405.2 3.0 copy-start.16
  405.2 4.2 copy-start.37
  405.2 251.3 %copy-start.6 = (f32[256,1024]{1,0:T(8,128)S(1)}, f32[256,1024]{1,0:T(8,128)}, u32[]{:S(2)}) copy-start(f32[256,1024]{1,0:T(8,128)} %get-tuple-element.126) | copy-start | bytes 3145732
Sparse Core Ops, SparseCore 0:
  103.5 20.3 reduce-scatter.5
  141.5 23.7 reduce-scatter.7
  193.4 23.5 reduce-scatter.9
  235.0 23.7 reduce-scatter.11
  278.2 166.7 reduce-scatter.13
